TPU v7x, 1024 devices: a whole 4x4x32 slice. The times are simulated.
1024 devices in a mesh: lat: 32 (over y, x, core), lev: 32 (over z).
Axes of the slice: x: 4, y: 4, z: 32, core: 2. Of those that a mesh axis runs over, the one named last changes fastest.
Arguments:
- tracers: float32 [3, 64, 256, 2880], P(None, 'lev', 'lat'), may hold values from -6 to 6
- courant_x: float32 [64, 256, 2880], P('lev', 'lat'), may hold values from -0.8 to 0.8
- courant_y: float32 [64, 256, 2880], P('lev', 'lat'), may hold values from -0.8 to 0.8
- thickness: float32 [256, 2880, 64], P('lat', 'lev'), may hold values from 0.5 to 5
- targets: int32 [256, 2880, 64], P('lat', 'lev'), may hold values from 0 to 31, never falling along the last dimension, each value on 1 to 4 neighbouring positions
Outputs:
- remapped: float32 [3, 32, 256, 2880], P(None, 'lev', 'lat')
Inputs may be any that keep to these rules, and one draw needn't show every extreme that they name: Along the levels of each column the targets never fall; each of the 32 new levels receives 1 to 4 source levels, and in each column one receives exactly 4.
All inputs are finite; a program needn't handle non-finite values.
Results may differ from a plain program's by a relative error of at most 0.0003.
Values sent between devices are 32-bit elements; how exact they have to be, the bound alone decides.
No kernel may reach another device: no remote copies, remote signals or barrier semaphores. Data moves between devices by JAX's collectives and lax.ppermute only.
A program may use at most 64 MiB of HBM per device.

v0:
```python
import jax
import jax.numpy as jnp
from jax import lax
from jax.sharding import PartitionSpec as P

SUBSTEPS = 2


def padded_2(cells, sides, width):
    for axis, dim in sides:
        count = lax.axis_size(axis)
        ends = count - 1
        head = lax.slice_in_dim(cells, 0, width, axis=dim)
        tail = lax.slice_in_dim(cells, cells.shape[dim] - width, cells.shape[dim], axis=dim)
        cells = jnp.concatenate(
            [
                lax.ppermute(tail, axis, [(i, (i + 1) % count) for i in range(ends)]),
                cells,
                lax.ppermute(head, axis, [((i + 1) % count, i) for i in range(ends)]),
            ],
            axis=dim,
        )
    return cells


def ppm_sweep(padded, faces, axis, count):

    def piece(start, stop):
        return lax.slice_in_dim(padded, start, stop, axis=axis)

    face_val = 7.0 / 12.0 * (piece(1, count + 4) + piece(2, count + 5)) - 1.0 / 12.0 * (
        piece(0, count + 3) + piece(3, count + 6)
    )
    cell_midpoint = piece(2, count + 4)
    left_face = lax.slice_in_dim(face_val, 0, count + 2, axis=axis)
    right_face = lax.slice_in_dim(face_val, 1, count + 3, axis=axis)
    slope = right_face - left_face
    curve = 6.0 * (cell_midpoint - 0.5 * (left_face + right_face))

    def lower(x):
        return lax.slice_in_dim(x, 0, count + 1, axis=axis)

    def upper(x):
        return lax.slice_in_dim(x, 1, count + 2, axis=axis)

    from_left = lower(right_face) - 0.5 * faces * (
        lower(slope) - (1.0 - 2.0 * faces / 3.0) * lower(curve)
    )
    from_right = upper(left_face) - 0.5 * faces * (
        upper(slope) + (1.0 + 2.0 * faces / 3.0) * upper(curve)
    )
    flux = faces * jnp.where(faces > 0, from_left, from_right)
    inner = piece(3, count + 3)
    return inner - (
        lax.slice_in_dim(flux, 1, count + 1, axis=axis)
        - lax.slice_in_dim(flux, 0, count, axis=axis)
    )


def lon_sweep(field, courant_x):
    count = field.shape[-1]
    padded = jnp.concatenate([field[..., -3:], field, field[..., :3]], axis=-1)
    faces = jnp.concatenate([courant_x[..., -1:], courant_x], axis=-1)
    return ppm_sweep(padded, faces, 3, count)


def lat_sweep(padded, faces, first_row, total_rows):
    count = padded.shape[2] - 6
    face_rows = first_row - 1 + jnp.arange(count + 1, dtype=jnp.int32)
    valid = ((face_rows >= 0) & (face_rows <= total_rows - 2)).astype(jnp.float32)
    faces = faces * valid[None, :, None]
    swept = ppm_sweep(padded, faces, 2, count)
    cell_rows = first_row + jnp.arange(count, dtype=jnp.int32)
    inside = ((cell_rows >= 0) & (cell_rows < total_rows)).astype(jnp.float32)
    return swept * inside[None, None, :, None]


def remap_columns(adv, thick, tg, levels_out):
    ks = jnp.arange(levels_out, dtype=jnp.int32)
    member = tg[None] == ks[:, None, None, None]
    mass = adv * thick[None]
    new_mass = jnp.sum(jnp.where(member[None], mass[:, None], 0.0), axis=2)
    new_thick = jnp.sum(jnp.where(member, thick[None], 0.0), axis=1)
    return jnp.transpose(new_mass / new_thick[None], (1, 0, 2, 3))


def local(tracers, courant_x, courant_y, thickness, targets):
    rows = tracers.shape[2]
    kinds = tracers.shape[0]
    total_rows = rows * lax.axis_size("lat")
    first_row = lax.axis_index("lat") * rows
    parts = lax.axis_size("lev")
    lon = tracers.shape[3]
    width = lon // parts
    levels_out = tracers.shape[1] * parts // 2
    field = tracers
    for step in range(SUBSTEPS):
        field = lon_sweep(field, courant_x)
        stacked = jnp.concatenate([field, courant_y[None]], axis=0)
        padded = padded_2(stacked, (("lat", 2),), 3)
        field = lat_sweep(padded[:kinds], padded[kinds][:, 2 : rows + 3], first_row, total_rows)
    blocks = jnp.transpose(field.reshape(field.shape[:3] + (parts, width)), (3, 0, 1, 2, 4))
    got = lax.all_to_all(blocks.reshape(parts, -1), "lev", split_axis=0, concat_axis=0, tiled=True).reshape(blocks.shape)
    adv = jnp.transpose(got, (1, 0, 2, 3, 4)).reshape(kinds, -1, rows, width)
    thick = jnp.transpose(thickness, (2, 0, 1))
    tg = jnp.transpose(targets, (2, 0, 1))
    out = remap_columns(adv, thick, tg, levels_out)
    back = lax.all_to_all(out.reshape(parts, -1), "lev", split_axis=0, concat_axis=0, tiled=True).reshape(out.shape)
    return jnp.transpose(back, (1, 2, 0, 3)).reshape(kinds, 1, rows, lon)


def solution(mesh):
    placed = (
        P(None, "lev", "lat", None),
        P("lev", "lat", None),
        P("lev", "lat", None),
        P("lat", "lev", None),
        P("lat", "lev", None),
    )
    return jax.shard_map(
        local, mesh=mesh, in_specs=placed, out_specs=P(None, "lev", "lat", None), check_vma=False
    )
```

profile of v0, /device:TPU:7, one launch (start us, length us, event | category | flops | bytes accessed | tf_op | source)
XLA Modules:
  0.0 209.9 jit_solution(571845386127110589)
XLA Ops:
  2.5 1.3 concatenate.58
  3.8 1.8 fusion.59
  7.3 2.0 fusion.62
  10.6 3.7 %collective-permute-start = (f32[4,2,3,2880]{3,0,2,1:T(4,128)S(1)}, f32[4,2,3,2880]{3,0,2,1:T(4,128)S(1)}, u32[]{:S(2)}, u32[]{:S(2)}) collective-permute-start(f32[4,2,3,2880]{3,0,2,1:T(4,128)S(1)} %copy.84), channel_id=1, source_target_pairs={{0,32},{32,64},{64,96},{96,128},{128,160},{160,192},{192,224},{224... | collective-permute-start | bytes 829448 | tf_op jit(solution)/shard_map/ppermute | solution.py:17
  14.4 2.1 %collective-permute-start.1 = (f32[4,2,3,2880]{3,0,2,1:T(4,128)S(1)}, f32[4,2,3,2880]{3,0,2,1:T(4,128)S(1)}, u32[]{:S(2)}, u32[]{:S(2)}) collective-permute-start(f32[4,2,3,2880]{3,0,2,1:T(4,128)S(1)} %copy.85), channel_id=1, source_target_pairs={{32,0},{64,32},{96,64},{128,96},{160,128},{192,160},{224,192},{256... | collective-permute-start | bytes 829448 | tf_op jit(solution)/shard_map/ppermute | solution.py:19
  16.6 1.3 collective-permute-done
  18.0 6.4 %collective-permute-done.1 = f32[4,2,3,2880]{3,0,2,1:T(4,128)S(1)} collective-permute-done((f32[4,2,3,2880]{3,0,2,1:T(4,128)S(1)}, f32[4,2,3,2880]{3,0,2,1:T(4,128)S(1)}, u32[]{:S(2)}, u32[]{:S(2)}) %collective-permute-start.1) | collective-permute-done | bytes 276512 | tf_op jit(solution)/shard_map/ppermute | solution.py:19
  25.2 1.5 fusion.7
  29.4 1.3 concatenate.65
  30.8 1.8 fusion.46
  32.6 1.2 slice_subtract_fusion.10
  33.8 1.9 fusion.63
  36.7 1.9 collective-permute-start.2
  38.7 2.6 %collective-permute-start.3 = (f32[4,2,3,2880]{3,0,2,1:T(4,128)S(1)}, f32[4,2,3,2880]{3,0,2,1:T(4,128)S(1)}, u32[]{:S(2)}, u32[]{:S(2)}) collective-permute-start(f32[4,2,3,2880]{3,0,2,1:T(4,128)S(1)} %copy.92), channel_id=1, source_target_pairs={{32,0},{64,32},{96,64},{128,96},{160,128},{192,160},{224,192},{256... | collective-permute-start | bytes 829448 | tf_op jit(solution)/shard_map/ppermute | solution.py:19
  42.3 6.4 %collective-permute-done.3 = f32[4,2,3,2880]{3,0,2,1:T(4,128)S(1)} collective-permute-done((f32[4,2,3,2880]{3,0,2,1:T(4,128)S(1)}, f32[4,2,3,2880]{3,0,2,1:T(4,128)S(1)}, u32[]{:S(2)}, u32[]{:S(2)}) %collective-permute-start.3) | collective-permute-done | bytes 276512 | tf_op jit(solution)/shard_map/ppermute | solution.py:19
  49.5 1.5 fusion.11
  53.7 1.4 reshape.103
  55.5 2.2 %all_to_all.16 = f32[32,1,4320]{2,1,0:T(1,128)} reshape(f32[32,3,2,8,90]{4,3,2,1,0:T(8,128)S(1)} %copy.98) | data formatting | bytes 1105920 | tf_op jit(solution)/shard_map/all_to_all | solution.py:103
  57.7 28.8 %all-to-all-start = ((f32[32,1,4320]{2,1,0:T(1,128)}), f32[32,1,4320]{2,1,0:T(1,128)}, u32[]{:S(2)}, u32[]{:S(2)}) async-start(f32[32,1,4320]{2,1,0:T(1,128)} %all_to_all.16), calls=%async_computation | async-start | bytes 1114112 | tf_op jit(solution)/shard_map/all_to_all | solution.py:103
  89.2 62.3 %all-to-all-done = f32[32,1,4320]{2,1,0:T(1,128)} async-done(((f32[32,1,4320]{2,1,0:T(1,128)}), f32[32,1,4320]{2,1,0:T(1,128)}, u32[]{:S(2)}, u32[]{:S(2)}) %all-to-all-start) | async-done | bytes 552992 | tf_op jit(solution)/shard_map/all_to_all | solution.py:103
  151.5 3.2 %reduce = f32[32,4320]{1,0:T(8,128)} reduce(f32[32,1,4320]{2,1,0:T(1,128)} %all-to-all-done, f32[]{:T(128)} %constant.54), dimensions={1}, to_apply=%all_to_all.13.reduce_sub_computation | reduce | bytes 1105924 | tf_op jit(solution)/shard_map/all_to_all | solution.py:103
  154.6 1.7 reshape.104
  156.5 3.9 %select_reduce_fusion = f32[3,32,8,90]{3,2,1,0:T(8,128)S(1)} fusion(f32[3,64,8,90]{3,2,1,0:T(8,128)S(1)} %broadcast_multiply_fusion, pred[32,64,8,90]{3,2,1,0:T(8,128)(4,1)S(1)} %iota_compare_fusion), kind=kLoop, calls=%fused_computation | loop fusion | flops 8778240 | bytes 2304000 | tf_op jit(solution)/shard_map/reduce_sum | solution.py:82
  161.0 47.0 %all_to_all.20 = f32[32,1,2160]{2,1,0:T(1,128)S(1)} all-to-all(f32[32,1,2160]{2,1,0:T(1,128)S(1)} %all_to_all.17), channel_id=1, replica_groups=mesh['lat'=32,'lev'=32] {'lev'}, dimensions={0} | all-to-all | bytes 552960 | tf_op jit(solution)/shard_map/all_to_all | solution.py:108
  (68 shorter events, 20.0 us)
Async XLA Ops:
  0.0 2.1 copy-start
  9.3 0.9 copy-start.3
  10.6 7.2 %collective-permute-start = (f32[4,2,3,2880]{3,0,2,1:T(4,128)S(1)}, f32[4,2,3,2880]{3,0,2,1:T(4,128)S(1)}, u32[]{:S(2)}, u32[]{:S(2)}) collective-permute-start(f32[4,2,3,2880]{3,0,2,1:T(4,128)S(1)} %copy.84), channel_id=1, source_target_pairs={{0,32},{32,64},{64,96},{96,128},{128,160},{160,192},{192,224},{224... | collective-permute-start | bytes 829448 | tf_op jit(solution)/shard_map/ppermute | solution.py:17
  14.4 10.0 %collective-permute-start.1 = (f32[4,2,3,2880]{3,0,2,1:T(4,128)S(1)}, f32[4,2,3,2880]{3,0,2,1:T(4,128)S(1)}, u32[]{:S(2)}, u32[]{:S(2)}) collective-permute-start(f32[4,2,3,2880]{3,0,2,1:T(4,128)S(1)} %copy.85), channel_id=1, source_target_pairs={{32,0},{64,32},{96,64},{128,96},{160,128},{192,160},{224,192},{256... | collective-permute-start | bytes 829448 | tf_op jit(solution)/shard_map/ppermute | solution.py:19
  36.7 5.4 %collective-permute-start.2 = (f32[4,2,3,2880]{3,0,2,1:T(4,128)S(1)}, f32[4,2,3,2880]{3,0,2,1:T(4,128)S(1)}, u32[]{:S(2)}, u32[]{:S(2)}) collective-permute-start(f32[4,2,3,2880]{3,0,2,1:T(4,128)S(1)} %copy.91), channel_id=1, source_target_pairs={{0,32},{32,64},{64,96},{96,128},{128,160},{160,192},{192,224},{224... | collective-permute-start | bytes 829448 | tf_op jit(solution)/shard_map/ppermute | solution.py:17
  38.7 10.0 %collective-permute-start.3 = (f32[4,2,3,2880]{3,0,2,1:T(4,128)S(1)}, f32[4,2,3,2880]{3,0,2,1:T(4,128)S(1)}, u32[]{:S(2)}, u32[]{:S(2)}) collective-permute-start(f32[4,2,3,2880]{3,0,2,1:T(4,128)S(1)} %copy.92), channel_id=1, source_target_pairs={{32,0},{64,32},{96,64},{128,96},{160,128},{192,160},{224,192},{256... | collective-permute-start | bytes 829448 | tf_op jit(solution)/shard_map/ppermute | solution.py:19
  55.5 31.0 %copy-start.1 = (f32[8,90,64]{1,2,0:T(8,128)S(1)}, f32[8,90,64]{1,2,0:T(8,128)}, u32[]{:S(2)}) copy-start(f32[8,90,64]{1,2,0:T(8,128)} %param.8) | copy-start | bytes 552964
  55.5 31.2 %copy-start.2 = (s32[8,90,64]{1,2,0:T(8,128)S(1)}, s32[8,90,64]{1,2,0:T(8,128)}, u32[]{:S(2)}) copy-start(s32[8,90,64]{1,2,0:T(8,128)} %param.9) | copy-start | bytes 552964
  57.7 93.8 %all-to-all-start = ((f32[32,1,4320]{2,1,0:T(1,128)}), f32[32,1,4320]{2,1,0:T(1,128)}, u32[]{:S(2)}, u32[]{:S(2)}) async-start(f32[32,1,4320]{2,1,0:T(1,128)} %all_to_all.16), calls=%async_computation | async-start | bytes 1114112 | tf_op jit(solution)/shard_map/all_to_all | solution.py:103
where the time goes:
time: 210 us
  waiting for transfers between devices  77.3 us (37%)
  blocking collectives  47 us (22%)
  starting transfers between devices  39.2 us (19%)
  other arithmetic  32.3 us (15%)
  local copies, waits for them, and re-layouts  13.7 us (7%)
    all_to_all x1, waiting for transfers between devices, local(): lax.all_to_all(blocks.reshape(parts, -1), 'lev', split_axis=0, concat_axi...  62.3 us
    all_to_all x1, blocking collectives, local(): lax.all_to_all(out.reshape(parts, -1), 'lev', split_axis=0, concat_axis=0...  47 us
    all_to_all x1, starting transfers between devices, local(): lax.all_to_all(blocks.reshape(parts, -1), 'lev', split_axis=0, concat_axi...  28.8 us
    ppermute x2, waiting for transfers between devices, padded_2(): lax.ppermute(head, axis, [((i + 1) % count, i) for i in range(ends)])  12.9 us
    sub x4, other arithmetic, ppm_sweep(): 7.0 / 12.0 * (piece(1, count + 4) + piece(2, count + 5))  6.65 us
    mul x4, other arithmetic, ppm_sweep(): flux = faces * jnp.where(faces > 0, from_left, from_right)  5.94 us
    ppermute x2, starting transfers between devices, padded_2(): lax.ppermute(tail, axis, [(i, (i + 1) % count) for i in range(ends)])  5.6 us
    ppermute x2, starting transfers between devices, padded_2(): lax.ppermute(head, axis, [((i + 1) % count, i) for i in range(ends)])  4.73 us
  transfers between devices with their start and end apart: 5, of which 5 were waited for; matrix products, arithmetic and copies ran while one was open for 1% of the time, Pallas kernels for 0%

commit v1 on v0

--- a/solution.py
+++ b/solution.py
@@ -76,11 +76,14 @@
 
 
 def remap_columns(adv, thick, tg, levels_out):
-    ks = jnp.arange(levels_out, dtype=jnp.int32)
-    member = tg[None] == ks[:, None, None, None]
+    ks = jnp.arange(levels_out, dtype=jnp.int32)[:, None, None]
     mass = adv * thick[None]
-    new_mass = jnp.sum(jnp.where(member[None], mass[:, None], 0.0), axis=2)
-    new_thick = jnp.sum(jnp.where(member, thick[None], 0.0), axis=1)
+    new_mass = 0.0
+    new_thick = 0.0
+    for shift in range(tg.shape[0] - levels_out + 1):
+        member = tg[shift : shift + levels_out] == ks
+        new_mass = new_mass + jnp.where(member[None], mass[:, shift : shift + levels_out], 0.0)
+        new_thick = new_thick + jnp.where(member, thick[shift : shift + levels_out], 0.0)
     return jnp.transpose(new_mass / new_thick[None], (1, 0, 2, 3))
 
 

time: 210 us -> 205 us (0.976)
  other arithmetic: 32.3 us -> 27.8 us
    reduce_sum x2 -> x0, other arithmetic: 4.93 us -> none  [the longest x1 3.85 us: remap_columns(): new_mass = jnp.sum(jnp.where(member[None], mass[:, None], 0.0), axis=2)]
where the time goes in v1:
time: 205 us
  waiting for transfers between devices  77.1 us (38%)
  blocking collectives  47 us (23%)
  starting transfers between devices  39 us (19%)
  other arithmetic  27.8 us (14%)
  local copies, waits for them, and re-layouts  13.3 us (6%)
    all_to_all x1, waiting for transfers between devices, local(): lax.all_to_all(blocks.reshape(parts, -1), 'lev', split_axis=0, concat_axi...  62.1 us
    all_to_all x1, blocking collectives, local(): lax.all_to_all(out.reshape(parts, -1), 'lev', split_axis=0, concat_axis=0...  47 us
    all_to_all x1, starting transfers between devices, local(): lax.all_to_all(blocks.reshape(parts, -1), 'lev', split_axis=0, concat_axi...  28.7 us
    ppermute x2, waiting for transfers between devices, padded_2(): lax.ppermute(head, axis, [((i + 1) % count, i) for i in range(ends)])  12.9 us
    sub x4, other arithmetic, ppm_sweep(): 7.0 / 12.0 * (piece(1, count + 4) + piece(2, count + 5))  6.66 us
    mul x4, other arithmetic, ppm_sweep(): flux = faces * jnp.where(faces > 0, from_left, from_right)  5.99 us
    ppermute x2, starting transfers between devices, padded_2(): lax.ppermute(tail, axis, [(i, (i + 1) % count) for i in range(ends)])  5.6 us
    ppermute x2, starting transfers between devices, padded_2(): lax.ppermute(head, axis, [((i + 1) % count, i) for i in range(ends)])  4.73 us
  transfers between devices with their start and end apart: 5, of which 5 were waited for; matrix products, arithmetic and copies ran while one was open for 1% of the time, Pallas kernels for 0%

profile of v1, /device:TPU:7, one launch (start us, length us, event | category | flops | bytes accessed | tf_op | source)
XLA Modules:
  0.0 205.0 jit_solution(9688354443180210882)
XLA Ops:
  2.5 1.3 concatenate.58
  3.8 1.8 fusion.59
  5.6 1.2 slice_subtract_fusion.11
  7.3 1.9 fusion.62
  10.6 3.7 %collective-permute-start = (f32[4,2,3,2880]{3,0,2,1:T(4,128)S(1)}, f32[4,2,3,2880]{3,0,2,1:T(4,128)S(1)}, u32[]{:S(2)}, u32[]{:S(2)}) collective-permute-start(f32[4,2,3,2880]{3,0,2,1:T(4,128)S(1)} %copy.179), channel_id=1, source_target_pairs={{0,32},{32,64},{64,96},{96,128},{128,160},{160,192},{192,224},{224... | collective-permute-start | bytes 829448 | tf_op jit(solution)/shard_map/ppermute | solution.py:17
  14.4 2.1 %collective-permute-start.1 = (f32[4,2,3,2880]{3,0,2,1:T(4,128)S(1)}, f32[4,2,3,2880]{3,0,2,1:T(4,128)S(1)}, u32[]{:S(2)}, u32[]{:S(2)}) collective-permute-start(f32[4,2,3,2880]{3,0,2,1:T(4,128)S(1)} %copy.180), channel_id=1, source_target_pairs={{32,0},{64,32},{96,64},{128,96},{160,128},{192,160},{224,192},{256... | collective-permute-start | bytes 829448 | tf_op jit(solution)/shard_map/ppermute | solution.py:19
  16.5 1.3 collective-permute-done
  18.0 6.4 %collective-permute-done.1 = f32[4,2,3,2880]{3,0,2,1:T(4,128)S(1)} collective-permute-done((f32[4,2,3,2880]{3,0,2,1:T(4,128)S(1)}, f32[4,2,3,2880]{3,0,2,1:T(4,128)S(1)}, u32[]{:S(2)}, u32[]{:S(2)}) %collective-permute-start.1) | collective-permute-done | bytes 276512 | tf_op jit(solution)/shard_map/ppermute | solution.py:19
  25.2 1.5 fusion.7
  29.4 1.3 concatenate.65
  30.7 1.8 fusion.46
  33.8 1.9 fusion.63
  36.7 1.9 collective-permute-start.2
  38.8 2.6 %collective-permute-start.3 = (f32[4,2,3,2880]{3,0,2,1:T(4,128)S(1)}, f32[4,2,3,2880]{3,0,2,1:T(4,128)S(1)}, u32[]{:S(2)}, u32[]{:S(2)}) collective-permute-start(f32[4,2,3,2880]{3,0,2,1:T(4,128)S(1)} %copy.187), channel_id=1, source_target_pairs={{32,0},{64,32},{96,64},{128,96},{160,128},{192,160},{224,192},{256... | collective-permute-start | bytes 829448 | tf_op jit(solution)/shard_map/ppermute | solution.py:19
  42.3 6.4 %collective-permute-done.3 = f32[4,2,3,2880]{3,0,2,1:T(4,128)S(1)} collective-permute-done((f32[4,2,3,2880]{3,0,2,1:T(4,128)S(1)}, f32[4,2,3,2880]{3,0,2,1:T(4,128)S(1)}, u32[]{:S(2)}, u32[]{:S(2)}) %collective-permute-start.3) | collective-permute-done | bytes 276512 | tf_op jit(solution)/shard_map/ppermute | solution.py:19
  49.5 1.5 fusion.11
  53.7 1.4 reshape.125
  55.5 2.2 %all_to_all.16 = f32[32,1,4320]{2,1,0:T(1,128)} reshape(f32[32,3,2,8,90]{4,3,2,1,0:T(8,128)S(1)} %copy.193) | data formatting | bytes 1105920 | tf_op jit(solution)/shard_map/all_to_all | solution.py:106
  57.7 28.7 %all-to-all-start = ((f32[32,1,4320]{2,1,0:T(1,128)}), f32[32,1,4320]{2,1,0:T(1,128)S(1)}, u32[]{:S(2)}, u32[]{:S(2)}) async-start(f32[32,1,4320]{2,1,0:T(1,128)} %all_to_all.16), calls=%async_computation | async-start | bytes 1114112 | tf_op jit(solution)/shard_map/all_to_all | solution.py:106
  86.6 1.6 fusion.100
  89.2 62.1 %all-to-all-done = f32[32,1,4320]{2,1,0:T(1,128)S(1)} async-done(((f32[32,1,4320]{2,1,0:T(1,128)}), f32[32,1,4320]{2,1,0:T(1,128)S(1)}, u32[]{:S(2)}, u32[]{:S(2)}) %all-to-all-start) | async-done | bytes 552992 | tf_op jit(solution)/shard_map/all_to_all | solution.py:106
  151.4 1.3 reduce
  153.5 2.0 fusion.66
  156.1 47.0 %all_to_all.20 = f32[32,1,2160]{2,1,0:T(1,128)S(1)} all-to-all(f32[32,1,2160]{2,1,0:T(1,128)S(1)} %all_to_all.17), channel_id=1, replica_groups=mesh['lat'=32,'lev'=32] {'lev'}, dimensions={0} | all-to-all | bytes 552960 | tf_op jit(solution)/shard_map/all_to_all | solution.py:111
  (99 shorter events, 19.0 us)
Async XLA Ops:
  0.0 2.1 %copy-start.2 = (f32[3,2,8,2880]{3,2,1,0:T(8,128)S(1)}, f32[3,2,8,2880]{3,2,1,0:T(8,128)}, u32[]{:S(2)}) copy-start(f32[3,2,8,2880]{3,2,1,0:T(8,128)} %param.5) | copy-start | bytes 1658884
  9.2 0.9 copy-start.3
  10.6 7.2 %collective-permute-start = (f32[4,2,3,2880]{3,0,2,1:T(4,128)S(1)}, f32[4,2,3,2880]{3,0,2,1:T(4,128)S(1)}, u32[]{:S(2)}, u32[]{:S(2)}) collective-permute-start(f32[4,2,3,2880]{3,0,2,1:T(4,128)S(1)} %copy.179), channel_id=1, source_target_pairs={{0,32},{32,64},{64,96},{96,128},{128,160},{160,192},{192,224},{224... | collective-permute-start | bytes 829448 | tf_op jit(solution)/shard_map/ppermute | solution.py:17
  14.4 10.0 %collective-permute-start.1 = (f32[4,2,3,2880]{3,0,2,1:T(4,128)S(1)}, f32[4,2,3,2880]{3,0,2,1:T(4,128)S(1)}, u32[]{:S(2)}, u32[]{:S(2)}) collective-permute-start(f32[4,2,3,2880]{3,0,2,1:T(4,128)S(1)} %copy.180), channel_id=1, source_target_pairs={{32,0},{64,32},{96,64},{128,96},{160,128},{192,160},{224,192},{256... | collective-permute-start | bytes 829448 | tf_op jit(solution)/shard_map/ppermute | solution.py:19
  36.7 5.4 %collective-permute-start.2 = (f32[4,2,3,2880]{3,0,2,1:T(4,128)S(1)}, f32[4,2,3,2880]{3,0,2,1:T(4,128)S(1)}, u32[]{:S(2)}, u32[]{:S(2)}) collective-permute-start(f32[4,2,3,2880]{3,0,2,1:T(4,128)S(1)} %copy.186), channel_id=1, source_target_pairs={{0,32},{32,64},{64,96},{96,128},{128,160},{160,192},{192,224},{224... | collective-permute-start | bytes 829448 | tf_op jit(solution)/shard_map/ppermute | solution.py:17
  38.8 10.0 %collective-permute-start.3 = (f32[4,2,3,2880]{3,0,2,1:T(4,128)S(1)}, f32[4,2,3,2880]{3,0,2,1:T(4,128)S(1)}, u32[]{:S(2)}, u32[]{:S(2)}) collective-permute-start(f32[4,2,3,2880]{3,0,2,1:T(4,128)S(1)} %copy.187), channel_id=1, source_target_pairs={{32,0},{64,32},{96,64},{128,96},{160,128},{192,160},{224,192},{256... | collective-permute-start | bytes 829448 | tf_op jit(solution)/shard_map/ppermute | solution.py:19
  55.5 30.9 %copy-start = (f32[8,90,64]{1,2,0:T(8,128)S(1)}, f32[8,90,64]{1,2,0:T(8,128)}, u32[]{:S(2)}) copy-start(f32[8,90,64]{1,2,0:T(8,128)} %param.8) | copy-start | bytes 552964
  55.5 31.1 %copy-start.1 = (s32[8,90,64]{1,2,0:T(8,128)S(1)}, s32[8,90,64]{1,2,0:T(8,128)}, u32[]{:S(2)}) copy-start(s32[8,90,64]{1,2,0:T(8,128)} %param.9) | copy-start | bytes 552964
  57.7 93.7 %all-to-all-start = ((f32[32,1,4320]{2,1,0:T(1,128)}), f32[32,1,4320]{2,1,0:T(1,128)S(1)}, u32[]{:S(2)}, u32[]{:S(2)}) async-start(f32[32,1,4320]{2,1,0:T(1,128)} %all_to_all.16), calls=%async_computation | async-start | bytes 1114112 | tf_op jit(solution)/shard_map/all_to_all | solution.py:106

commit v2 on v1

--- a/solution.py
+++ b/solution.py
@@ -97,11 +97,15 @@
     width = lon // parts
     levels_out = tracers.shape[1] * parts // 2
     field = tracers
+    faces_y = None
     for step in range(SUBSTEPS):
         field = lon_sweep(field, courant_x)
-        stacked = jnp.concatenate([field, courant_y[None]], axis=0)
-        padded = padded_2(stacked, (("lat", 2),), 3)
-        field = lat_sweep(padded[:kinds], padded[kinds][:, 2 : rows + 3], first_row, total_rows)
+        if faces_y is None:
+            padded = padded_2(jnp.concatenate([field, courant_y[None]], axis=0), (("lat", 2),), 3)
+            faces_y = padded[kinds][:, 2 : rows + 3]
+        else:
+            padded = padded_2(field, (("lat", 2),), 3)
+        field = lat_sweep(padded[:kinds], faces_y, first_row, total_rows)
     blocks = jnp.transpose(field.reshape(field.shape[:3] + (parts, width)), (3, 0, 1, 2, 4))
     got = lax.all_to_all(blocks.reshape(parts, -1), "lev", split_axis=0, concat_axis=0, tiled=True).reshape(blocks.shape)
     adv = jnp.transpose(got, (1, 0, 2, 3, 4)).reshape(kinds, -1, rows, width)

time: 205 us -> 200 us (0.976)
  other arithmetic: 27.8 us -> 21 us
where the time goes in v2:
time: 200 us
  waiting for transfers between devices  77.6 us (39%)
  blocking collectives  47.3 us (24%)
  starting transfers between devices  38.8 us (19%)
  other arithmetic  21 us (10%)
  local copies, waits for them, and re-layouts  14.1 us (7%)
    all_to_all x1, waiting for transfers between devices, local(): lax.all_to_all(blocks.reshape(parts, -1), 'lev', split_axis=0, concat_axi...  62.4 us
    all_to_all x1, blocking collectives, local(): lax.all_to_all(out.reshape(parts, -1), 'lev', split_axis=0, concat_axis=0...  47.3 us
    all_to_all x1, starting transfers between devices, local(): lax.all_to_all(blocks.reshape(parts, -1), 'lev', split_axis=0, concat_axi...  28.5 us
    ppermute x2, waiting for transfers between devices, padded_2(): lax.ppermute(head, axis, [((i + 1) % count, i) for i in range(ends)])  13 us
    ppermute x2, starting transfers between devices, padded_2(): lax.ppermute(tail, axis, [(i, (i + 1) % count) for i in range(ends)])  5.6 us
    ppermute x2, starting transfers between devices, padded_2(): lax.ppermute(head, axis, [((i + 1) % count, i) for i in range(ends)])  4.73 us
    mul x4, other arithmetic, ppm_sweep(): flux = faces * jnp.where(faces > 0, from_left, from_right)  4.72 us
    sub x4, other arithmetic, ppm_sweep(): 7.0 / 12.0 * (piece(1, count + 4) + piece(2, count + 5))  4.69 us
  transfers between devices with their start and end apart: 5, of which 5 were waited for; matrix products, arithmetic and copies ran while one was open for 1% of the time, Pallas kernels for 0%

profile of v2, /device:TPU:7, one launch (start us, length us, event | category | flops | bytes accessed | tf_op | source)
XLA Modules:
  0.0 199.5 jit_solution(17758252136110737391)
XLA Ops:
  0.9 1.4 concatenate.55
  3.5 1.3 fusion.53
  5.4 1.3 fusion.46
  8.1 3.7 %collective-permute-start = (f32[4,2,3,2880]{3,0,2,1:T(4,128)S(1)}, f32[4,2,3,2880]{3,0,2,1:T(4,128)S(1)}, u32[]{:S(2)}, u32[]{:S(2)}) collective-permute-start(f32[4,2,3,2880]{3,0,2,1:T(4,128)S(1)} %get-tuple-element.47), channel_id=1, source_target_pairs={{0,32},{32,64},{64,96},{96,128},{128,160},{160,192},{192,224},{224... | collective-permute-start | bytes 829448 | tf_op jit(solution)/shard_map/ppermute | solution.py:17
  11.8 2.1 %collective-permute-start.1 = (f32[4,2,3,2880]{3,0,2,1:T(4,128)S(1)}, f32[4,2,3,2880]{3,0,2,1:T(4,128)S(1)}, u32[]{:S(2)}, u32[]{:S(2)}) collective-permute-start(f32[4,2,3,2880]{3,0,2,1:T(4,128)S(1)} %get-tuple-element.48), channel_id=1, source_target_pairs={{32,0},{64,32},{96,64},{128,96},{160,128},{192,160},{224,192},{256... | collective-permute-start | bytes 829448 | tf_op jit(solution)/shard_map/ppermute | solution.py:19
  13.9 1.4 collective-permute-done
  15.3 6.5 %collective-permute-done.1 = f32[4,2,3,2880]{3,0,2,1:T(4,128)S(1)} collective-permute-done((f32[4,2,3,2880]{3,0,2,1:T(4,128)S(1)}, f32[4,2,3,2880]{3,0,2,1:T(4,128)S(1)}, u32[]{:S(2)}, u32[]{:S(2)}) %collective-permute-start.1) | collective-permute-done | bytes 276512 | tf_op jit(solution)/shard_map/ppermute | solution.py:19
  24.7 1.0 fusion.21
  26.7 1.6 concatenate.62
  28.3 2.0 %fusion.38 = f32[3,2,8,2883]{3,0,2,1:T(4,128)S(1)} fusion(f32[3,2,8,2886]{3,0,2,1:T(4,128)S(1)} %concatenate.62, f32[3,2,8,2880]{3,0,2,1:T(4,128)S(1)} %fusion.40, f32[3,2,8,3]{3,0,2,1:T(4,128)} %get-tuple-element.54, f32[3,2,8,3]{3,0,2,1:T(4,128)} %get-tuple-element.53), kind=kLoop, calls=%fused_computation.61 | loop fusion | flops 968688 | bytes 2214720 | tf_op jit(solution)/shard_map/sub | solution.py:31
  31.4 1.3 fusion.32
  33.3 1.9 collective-permute-start.2
  35.2 2.6 %collective-permute-start.3 = (f32[3,2,3,2880]{3,0,2,1:T(4,128)S(1)}, f32[3,2,3,2880]{3,0,2,1:T(4,128)S(1)}, u32[]{:S(2)}, u32[]{:S(2)}) collective-permute-start(f32[3,2,3,2880]{3,0,2,1:T(4,128)S(1)} %get-tuple-element.50), channel_id=1, source_target_pairs={{32,0},{64,32},{96,64},{128,96},{160,128},{192,160},{224,192},{256... | collective-permute-start | bytes 622088 | tf_op jit(solution)/shard_map/ppermute | solution.py:19
  38.7 6.5 %collective-permute-done.3 = f32[3,2,3,2880]{3,0,2,1:T(4,128)S(1)} collective-permute-done((f32[3,2,3,2880]{3,0,2,1:T(4,128)S(1)}, f32[3,2,3,2880]{3,0,2,1:T(4,128)S(1)}, u32[]{:S(2)}, u32[]{:S(2)}) %collective-permute-start.3) | collective-permute-done | bytes 207392 | tf_op jit(solution)/shard_map/ppermute | solution.py:19
  46.5 1.0 fusion.13
  47.9 1.4 reshape.121
  49.8 2.2 %all_to_all.16 = f32[32,1,4320]{2,1,0:T(1,128)} reshape(f32[32,3,2,8,90]{4,3,2,1,0:T(8,128)S(1)} %copy.310) | data formatting | bytes 1105920 | tf_op jit(solution)/shard_map/all_to_all | solution.py:110
  52.0 28.5 %all-to-all-start = ((f32[32,1,4320]{2,1,0:T(1,128)}), f32[32,1,4320]{2,1,0:T(1,128)S(1)}, u32[]{:S(2)}, u32[]{:S(2)}) async-start(f32[32,1,4320]{2,1,0:T(1,128)} %all_to_all.16), calls=%async_computation | async-start | bytes 1114112 | tf_op jit(solution)/shard_map/all_to_all | solution.py:110
  80.6 1.6 fusion.89
  83.2 62.4 %all-to-all-done = f32[32,1,4320]{2,1,0:T(1,128)S(1)} async-done(((f32[32,1,4320]{2,1,0:T(1,128)}), f32[32,1,4320]{2,1,0:T(1,128)S(1)}, u32[]{:S(2)}, u32[]{:S(2)}) %all-to-all-start) | async-done | bytes 552992 | tf_op jit(solution)/shard_map/all_to_all | solution.py:110
  145.6 1.3 reduce
  147.8 2.0 %fusion.57 = f32[32,3,8,90]{3,2,0,1:T(8,128)S(1)} fusion(f32[3,64,8,90]{3,2,1,0:T(8,128)S(1)} %broadcast_multiply_fusion, f32[32,8,90]{2,1,0:T(8,128)S(1)} %copy.346, pred[32,8,90]{2,1,0:T(8,128)(4,1)S(1)} %copy.345, pred[32,8,90]{2,1,0:T(8,128)(4,1)S(1)} %copy.344, pred[32,8,90]{2,1,0:T(8,128)(4,1)S(1)} %copy.343, pred[32,8,90]{2,1,0:T(8,128)(4,1)S(1)} %copy.342, ...), kind=kLoop, calls=%fused_computation.93 | loop fusion | flops 4561920 | bytes 10252800 | tf_op jit(solution)/shard_map/transpose | solution.py:87
  150.3 47.3 %all_to_all.20 = f32[32,1,2160]{2,1,0:T(1,128)S(1)} all-to-all(f32[32,1,2160]{2,1,0:T(1,128)S(1)} %all_to_all.17), channel_id=1, replica_groups=mesh['lat'=32,'lev'=32] {'lev'}, dimensions={0} | all-to-all | bytes 552960 | tf_op jit(solution)/shard_map/all_to_all | solution.py:115
  198.6 1.0 reshape.125
  (97 shorter events, 15.6 us)
Async XLA Ops:
  0.0 2.3 %copy-start.2 = (f32[3,2,8,2880]{3,2,1,0:T(8,128)S(1)}, f32[3,2,8,2880]{3,2,1,0:T(8,128)}, u32[]{:S(2)}) copy-start(f32[3,2,8,2880]{3,2,1,0:T(8,128)} %param.5) | copy-start | bytes 1658884
  2.3 0.9 copy-start.7
  3.5 1.9 copy-start.3
  3.5 1.9 copy-start.5
  6.7 0.9 copy-start.8
  8.1 7.2 %collective-permute-start = (f32[4,2,3,2880]{3,0,2,1:T(4,128)S(1)}, f32[4,2,3,2880]{3,0,2,1:T(4,128)S(1)}, u32[]{:S(2)}, u32[]{:S(2)}) collective-permute-start(f32[4,2,3,2880]{3,0,2,1:T(4,128)S(1)} %get-tuple-element.47), channel_id=1, source_target_pairs={{0,32},{32,64},{64,96},{96,128},{128,160},{160,192},{192,224},{224... | collective-permute-start | bytes 829448 | tf_op jit(solution)/shard_map/ppermute | solution.py:17
  11.8 10.0 %collective-permute-start.1 = (f32[4,2,3,2880]{3,0,2,1:T(4,128)S(1)}, f32[4,2,3,2880]{3,0,2,1:T(4,128)S(1)}, u32[]{:S(2)}, u32[]{:S(2)}) collective-permute-start(f32[4,2,3,2880]{3,0,2,1:T(4,128)S(1)} %get-tuple-element.48), channel_id=1, source_target_pairs={{32,0},{64,32},{96,64},{128,96},{160,128},{192,160},{224,192},{256... | collective-permute-start | bytes 829448 | tf_op jit(solution)/shard_map/ppermute | solution.py:19
  30.3 0.9 copy-start.4
  30.4 1.0 copy-start.6
  33.3 5.4 %collective-permute-start.2 = (f32[3,2,3,2880]{3,0,2,1:T(4,128)S(1)}, f32[3,2,3,2880]{3,0,2,1:T(4,128)S(1)}, u32[]{:S(2)}, u32[]{:S(2)}) collective-permute-start(f32[3,2,3,2880]{3,0,2,1:T(4,128)S(1)} %get-tuple-element.49), channel_id=1, source_target_pairs={{0,32},{32,64},{64,96},{96,128},{128,160},{160,192},{192,224},{224... | collective-permute-start | bytes 622088 | tf_op jit(solution)/shard_map/ppermute | solution.py:17
  35.2 10.0 %collective-permute-start.3 = (f32[3,2,3,2880]{3,0,2,1:T(4,128)S(1)}, f32[3,2,3,2880]{3,0,2,1:T(4,128)S(1)}, u32[]{:S(2)}, u32[]{:S(2)}) collective-permute-start(f32[3,2,3,2880]{3,0,2,1:T(4,128)S(1)} %get-tuple-element.50), channel_id=1, source_target_pairs={{32,0},{64,32},{96,64},{128,96},{160,128},{192,160},{224,192},{256... | collective-permute-start | bytes 622088 | tf_op jit(solution)/shard_map/ppermute | solution.py:19
  49.8 30.6 %copy-start = (f32[8,90,64]{1,2,0:T(8,128)S(1)}, f32[8,90,64]{1,2,0:T(8,128)}, u32[]{:S(2)}) copy-start(f32[8,90,64]{1,2,0:T(8,128)} %param.8) | copy-start | bytes 552964
  49.8 30.8 %copy-start.1 = (s32[8,90,64]{1,2,0:T(8,128)S(1)}, s32[8,90,64]{1,2,0:T(8,128)}, u32[]{:S(2)}) copy-start(s32[8,90,64]{1,2,0:T(8,128)} %param.9) | copy-start | bytes 552964
  52.0 93.7 %all-to-all-start = ((f32[32,1,4320]{2,1,0:T(1,128)}), f32[32,1,4320]{2,1,0:T(1,128)S(1)}, u32[]{:S(2)}, u32[]{:S(2)}) async-start(f32[32,1,4320]{2,1,0:T(1,128)} %all_to_all.16), calls=%async_computation | async-start | bytes 1114112 | tf_op jit(solution)/shard_map/all_to_all | solution.py:110

commit v3 on v2

--- a/solution.py
+++ b/solution.py
@@ -101,8 +101,12 @@
     for step in range(SUBSTEPS):
         field = lon_sweep(field, courant_x)
         if faces_y is None:
-            padded = padded_2(jnp.concatenate([field, courant_y[None]], axis=0), (("lat", 2),), 3)
-            faces_y = padded[kinds][:, 2 : rows + 3]
+            count = lax.axis_size("lat")
+            stacked = jnp.concatenate([field, courant_y[None]], axis=0)
+            south = lax.ppermute(stacked[:, :, rows - 3 :], "lat", [(i, i + 1) for i in range(count - 1)])
+            north = lax.ppermute(field[:, :, :3], "lat", [(i + 1, i) for i in range(count - 1)])
+            padded = jnp.concatenate([south[:kinds], field, north], axis=2)
+            faces_y = jnp.concatenate([south[kinds], courant_y], axis=1)[:, 2 : rows + 3]
         else:
             padded = padded_2(field, (("lat", 2),), 3)
         field = lat_sweep(padded[:kinds], faces_y, first_row, total_rows)

time: 200 us -> 192 us (0.960)
  other arithmetic: 21 us -> 13.8 us
    ppermute x2 -> x1, waiting for transfers between devices: 13 us -> 6.51 us  [padded_2(): lax.ppermute(head, axis, [((i + 1) % count, i) for i in range(ends)])]
    ppermute x0 -> x2, waiting for transfers between devices: none -> 6.45 us  [the longest x1 4.62 us: local(): lax.ppermute(field[:, :, :3], 'lat', [(i + 1, i) for i in range(count - 1)])]
    ppermute x0 -> x2, starting transfers between devices: none -> 5.59 us  [the longest x1 3.68 us: local(): lax.ppermute(stacked[:, :, rows - 3:], 'lat', [(i, i + 1) for i in range(...]
    ppermute x2 -> x1, starting transfers between devices: 5.6 us -> 1.92 us  [padded_2(): lax.ppermute(tail, axis, [(i, (i + 1) % count) for i in range(ends)])]
    mul x4, other arithmetic: 4.72 us -> 2.29 us  [ppm_sweep(): flux = faces * jnp.where(faces > 0, from_left, from_right)]
    ppermute x2 -> x1, starting transfers between devices: 4.73 us -> 2.41 us  [padded_2(): lax.ppermute(head, axis, [((i + 1) % count, i) for i in range(ends)])]
  transfers between devices with their start and end apart: 5 -> 5, of which waited for: 5 -> 5; matrix products, arithmetic and copies ran while one was open for 1% -> 2% of each run, Pallas kernels for 0% -> 0%
where the time goes in v3:
time: 192 us
  waiting for transfers between devices  76.3 us (40%)
  blocking collectives  47.1 us (25%)
  starting transfers between devices  38.7 us (20%)
  local copies, waits for them, and re-layouts  15.2 us (8%)
  other arithmetic  13.8 us (7%)
    all_to_all x1, waiting for transfers between devices, local(): lax.all_to_all(blocks.reshape(parts, -1), 'lev', split_axis=0, concat_axi...  62.2 us
    all_to_all x1, blocking collectives, local(): lax.all_to_all(out.reshape(parts, -1), 'lev', split_axis=0, concat_axis=0...  47.1 us
    all_to_all x1, starting transfers between devices, local(): lax.all_to_all(blocks.reshape(parts, -1), 'lev', split_axis=0, concat_axi...  28.8 us
    ppermute x1, waiting for transfers between devices, padded_2(): lax.ppermute(head, axis, [((i + 1) % count, i) for i in range(ends)])  6.51 us
    ppermute x1, waiting for transfers between devices, local(): lax.ppermute(field[:, :, :3], 'lat', [(i + 1, i) for i in range(count - 1)])  4.62 us
  transfers between devices with their start and end apart: 5, of which 5 were waited for; matrix products, arithmetic and copies ran while one was open for 2% of the time, Pallas kernels for 0%

profile of v3, /device:TPU:7, one launch (start us, length us, event | category | flops | bytes accessed | tf_op | source)
XLA Modules:
  0.0 191.7 jit_solution(16880360526301706792)
XLA Ops:
  0.0 0.9 fusion.123
  0.9 1.4 concatenate.58
  5.5 3.7 %collective-permute-start = (f32[4,2,3,2880]{3,2,1,0:T(4,128)S(1)}, f32[4,2,3,2880]{3,2,1,0:T(4,128)S(1)}, u32[]{:S(2)}, u32[]{:S(2)}) collective-permute-start(f32[4,2,3,2880]{3,2,1,0:T(4,128)S(1)} %pad_maximum_fusion.3), channel_id=1, source_target_pairs={{0,32},{32,64},{64,96},{96,128},{128,160},{160,192},{192,224},{224... | collective-permute-start | bytes 829448 | tf_op jit(solution)/shard_map/ppermute | solution.py:106
  9.2 0.7 slice.680
  10.0 1.9 collective-permute-start.1
  11.9 1.8 collective-permute-done
  13.7 0.7 copy-done.5
  15.6 4.6 %collective-permute-done.1 = f32[3,2,3,2880]{3,2,1,0:T(4,128)S(1)} collective-permute-done((f32[3,2,3,2880]{3,2,1,0:T(4,128)}, f32[3,2,3,2880]{3,2,1,0:T(4,128)S(1)}, u32[]{:S(2)}, u32[]{:S(2)}) %collective-permute-start.1) | collective-permute-done | bytes 207392 | tf_op jit(solution)/shard_map/ppermute | solution.py:107
  22.0 0.7 fusion.122
  22.7 1.1 concatenate.66
  23.8 1.3 fusion.37
  26.3 1.9 %collective-permute-start.2 = (f32[3,2,3,2880]{3,2,1,0:T(4,128)S(1)}, f32[3,2,3,2880]{3,2,1,0:T(4,128)S(1)}, u32[]{:S(2)}, u32[]{:S(2)}) collective-permute-start(f32[3,2,3,2880]{3,2,1,0:T(4,128)S(1)} %get-tuple-element.45), channel_id=1, source_target_pairs={{0,32},{32,64},{64,96},{96,128},{128,160},{160,192},{192,224},{224... | collective-permute-start | bytes 622088 | tf_op jit(solution)/shard_map/ppermute | solution.py:17
  28.2 2.4 %collective-permute-start.3 = (f32[3,2,3,2880]{3,2,1,0:T(4,128)S(1)}, f32[3,2,3,2880]{3,2,1,0:T(4,128)S(1)}, u32[]{:S(2)}, u32[]{:S(2)}) collective-permute-start(f32[3,2,3,2880]{3,2,1,0:T(4,128)S(1)} %get-tuple-element.46), channel_id=1, source_target_pairs={{32,0},{64,32},{96,64},{128,96},{160,128},{192,160},{224,192},{256... | collective-permute-start | bytes 622088 | tf_op jit(solution)/shard_map/ppermute | solution.py:19
  30.6 1.1 collective-permute-done.2
  31.7 6.5 %collective-permute-done.3 = f32[3,2,3,2880]{3,2,1,0:T(4,128)S(1)} collective-permute-done((f32[3,2,3,2880]{3,2,1,0:T(4,128)S(1)}, f32[3,2,3,2880]{3,2,1,0:T(4,128)S(1)}, u32[]{:S(2)}, u32[]{:S(2)}) %collective-permute-start.3) | collective-permute-done | bytes 207392 | tf_op jit(solution)/shard_map/ppermute | solution.py:19
  40.1 1.4 reshape.121
  41.9 2.2 %all_to_all.16 = f32[32,1,4320]{2,1,0:T(1,128)} reshape(f32[32,3,2,8,90]{4,3,2,1,0:T(8,128)S(1)} %bitcast.26) | data formatting | bytes 1105920 | tf_op jit(solution)/shard_map/all_to_all | solution.py:114
  44.1 28.8 %all-to-all-start = ((f32[32,1,4320]{2,1,0:T(1,128)}), f32[32,1,4320]{2,1,0:T(1,128)S(1)}, u32[]{:S(2)}, u32[]{:S(2)}) async-start(f32[32,1,4320]{2,1,0:T(1,128)} %all_to_all.16), calls=%async_computation | async-start | bytes 1114112 | tf_op jit(solution)/shard_map/all_to_all | solution.py:114
  73.0 1.6 fusion.89
  75.7 62.2 %all-to-all-done = f32[32,1,4320]{2,1,0:T(1,128)S(1)} async-done(((f32[32,1,4320]{2,1,0:T(1,128)}), f32[32,1,4320]{2,1,0:T(1,128)S(1)}, u32[]{:S(2)}, u32[]{:S(2)}) %all-to-all-start) | async-done | bytes 552992 | tf_op jit(solution)/shard_map/all_to_all | solution.py:114
  137.9 1.3 reduce
  140.0 2.0 %fusion.56 = f32[32,3,8,90]{3,2,0,1:T(8,128)S(1)} fusion(f32[3,64,8,90]{3,2,1,0:T(8,128)S(1)} %broadcast_multiply_fusion, f32[32,8,90]{2,1,0:T(8,128)S(1)} %copy.154, pred[32,8,90]{2,1,0:T(8,128)(4,1)S(1)} %copy.153, pred[32,8,90]{2,1,0:T(8,128)(4,1)S(1)} %copy.152, pred[32,8,90]{2,1,0:T(8,128)(4,1)S(1)} %copy.151, pred[32,8,90]{2,1,0:T(8,128)(4,1)S(1)} %copy.150, ...), kind=kLoop, calls=%fused_computation.88 | loop fusion | flops 4561920 | bytes 10252800 | tf_op jit(solution)/shard_map/transpose | solution.py:87
  142.6 47.1 %all_to_all.20 = f32[32,1,2160]{2,1,0:T(1,128)S(1)} all-to-all(f32[32,1,2160]{2,1,0:T(1,128)S(1)} %all_to_all.17), channel_id=1, replica_groups=mesh['lat'=32,'lev'=32] {'lev'}, dimensions={0} | all-to-all | bytes 552960 | tf_op jit(solution)/shard_map/all_to_all | solution.py:119
  190.7 1.0 reshape.125
  (87 shorter events, 12.7 us)
Async XLA Ops:
  0.0 2.3 %copy-start.2 = (f32[3,2,8,2880]{3,2,1,0:T(8,128)S(1)}, f32[3,2,8,2880]{3,2,1,0:T(8,128)}, u32[]{:S(2)}) copy-start(f32[3,2,8,2880]{3,2,1,0:T(8,128)} %param.5) | copy-start | bytes 1658884
  2.8 0.9 copy-start.7
  4.5 0.9 copy-start.3
  4.8 9.8 %copy-start.4 = (f32[2,8,2880]{2,1,0:T(8,128)S(1)}, f32[2,8,2880]{2,1,0:T(8,128)}, u32[]{:S(2)}) copy-start(f32[2,8,2880]{2,1,0:T(8,128)} %param.7) | copy-start | bytes 552964
  5.5 8.2 %collective-permute-start = (f32[4,2,3,2880]{3,2,1,0:T(4,128)S(1)}, f32[4,2,3,2880]{3,2,1,0:T(4,128)S(1)}, u32[]{:S(2)}, u32[]{:S(2)}) collective-permute-start(f32[4,2,3,2880]{3,2,1,0:T(4,128)S(1)} %pad_maximum_fusion.3), channel_id=1, source_target_pairs={{0,32},{32,64},{64,96},{96,128},{128,160},{160,192},{192,224},{224... | collective-permute-start | bytes 829448 | tf_op jit(solution)/shard_map/ppermute | solution.py:106
  10.0 10.2 %collective-permute-start.1 = (f32[3,2,3,2880]{3,2,1,0:T(4,128)}, f32[3,2,3,2880]{3,2,1,0:T(4,128)S(1)}, u32[]{:S(2)}, u32[]{:S(2)}) collective-permute-start(f32[3,2,3,2880]{3,2,1,0:T(4,128)} %slice.680), channel_id=1, source_target_pairs={{32,0},{64,32},{96,64},{128,96},{160,128},{192,160},{224,192},{256... | collective-permute-start | bytes 622088 | tf_op jit(solution)/shard_map/ppermute | solution.py:107
  13.7 0.7 copy-start.5
  14.5 1.0 copy-start.6
  26.3 5.4 %collective-permute-start.2 = (f32[3,2,3,2880]{3,2,1,0:T(4,128)S(1)}, f32[3,2,3,2880]{3,2,1,0:T(4,128)S(1)}, u32[]{:S(2)}, u32[]{:S(2)}) collective-permute-start(f32[3,2,3,2880]{3,2,1,0:T(4,128)S(1)} %get-tuple-element.45), channel_id=1, source_target_pairs={{0,32},{32,64},{64,96},{96,128},{128,160},{160,192},{192,224},{224... | collective-permute-start | bytes 622088 | tf_op jit(solution)/shard_map/ppermute | solution.py:17
  28.2 10.0 %collective-permute-start.3 = (f32[3,2,3,2880]{3,2,1,0:T(4,128)S(1)}, f32[3,2,3,2880]{3,2,1,0:T(4,128)S(1)}, u32[]{:S(2)}, u32[]{:S(2)}) collective-permute-start(f32[3,2,3,2880]{3,2,1,0:T(4,128)S(1)} %get-tuple-element.46), channel_id=1, source_target_pairs={{32,0},{64,32},{96,64},{128,96},{160,128},{192,160},{224,192},{256... | collective-permute-start | bytes 622088 | tf_op jit(solution)/shard_map/ppermute | solution.py:19
  41.9 31.0 %copy-start = (f32[8,90,64]{1,2,0:T(8,128)S(1)}, f32[8,90,64]{1,2,0:T(8,128)}, u32[]{:S(2)}) copy-start(f32[8,90,64]{1,2,0:T(8,128)} %param.8) | copy-start | bytes 552964
  44.1 28.9 %copy-start.1 = (s32[8,90,64]{1,2,0:T(8,128)S(1)}, s32[8,90,64]{1,2,0:T(8,128)}, u32[]{:S(2)}) copy-start(s32[8,90,64]{1,2,0:T(8,128)} %param.9) | copy-start | bytes 552964
  44.1 93.8 %all-to-all-start = ((f32[32,1,4320]{2,1,0:T(1,128)}), f32[32,1,4320]{2,1,0:T(1,128)S(1)}, u32[]{:S(2)}, u32[]{:S(2)}) async-start(f32[32,1,4320]{2,1,0:T(1,128)} %all_to_all.16), calls=%async_computation | async-start | bytes 1114112 | tf_op jit(solution)/shard_map/all_to_all | solution.py:114

commit v4 on v3

--- a/solution.py
+++ b/solution.py
@@ -99,6 +99,7 @@
     field = tracers
     faces_y = None
     for step in range(SUBSTEPS):
+        before = field
         field = lon_sweep(field, courant_x)
         if faces_y is None:
             count = lax.axis_size("lat")
@@ -108,7 +109,16 @@
             padded = jnp.concatenate([south[:kinds], field, north], axis=2)
             faces_y = jnp.concatenate([south[kinds], courant_y], axis=1)[:, 2 : rows + 3]
         else:
-            padded = padded_2(field, (("lat", 2),), 3)
+            count = lax.axis_size("lat")
+            south = lax.ppermute(
+                lon_sweep(before[:, :, rows - 3 :], courant_x[:, rows - 3 :]),
+                "lat",
+                [(i, i + 1) for i in range(count - 1)],
+            )
+            north = lax.ppermute(
+                lon_sweep(before[:, :, :3], courant_x[:, :3]), "lat", [(i + 1, i) for i in range(count - 1)]
+            )
+            padded = jnp.concatenate([south, field, north], axis=2)
         field = lat_sweep(padded[:kinds], faces_y, first_row, total_rows)
     blocks = jnp.transpose(field.reshape(field.shape[:3] + (parts, width)), (3, 0, 1, 2, 4))
     got = lax.all_to_all(blocks.reshape(parts, -1), "lev", split_axis=0, concat_axis=0, tiled=True).reshape(blocks.shape)

time: 192 us -> 197 us (1.026)
  other arithmetic: 13.8 us -> 20.8 us
  waiting for transfers between devices: 76.3 us -> 71.2 us
  local copies, waits for them, and re-layouts: 15.2 us -> 17.3 us
    ppermute x2, waiting for transfers between devices: 7.61 us -> 3.42 us  [the longest x1 3.42 us: local(): lax.ppermute(lon_sweep(before[:, :, :3], courant_x[:, :3]), 'lat', [(i +...]
    sub x4 -> x5, other arithmetic: 2.75 us -> 4.44 us  [ppm_sweep(): 7.0 / 12.0 * (piece(1, count + 4) + piece(2, count + 5))]
  transfers between devices with their start and end apart: 5 -> 5, of which waited for: 5 -> 3; matrix products, arithmetic and copies ran while one was open for 2% -> 5% of each run, Pallas kernels for 0% -> 0%
where the time goes in v4:
time: 197 us; the launch traced here: 196 us
  waiting for transfers between devices  71.2 us (36%)
  blocking collectives  47.3 us (24%)
  starting transfers between devices  38.9 us (20%)
  other arithmetic  20.8 us (11%)
  local copies, waits for them, and re-layouts  17.3 us (9%)
    all_to_all x1, waiting for transfers between devices, local(): lax.all_to_all(blocks.reshape(parts, -1), 'lev', split_axis=0, concat_axi...  62.3 us
    all_to_all x1, blocking collectives, local(): lax.all_to_all(out.reshape(parts, -1), 'lev', split_axis=0, concat_axis=0...  47.3 us
    all_to_all x1, starting transfers between devices, local(): lax.all_to_all(blocks.reshape(parts, -1), 'lev', split_axis=0, concat_axi...  28.8 us
    ppermute x1, waiting for transfers between devices, local(): lax.ppermute(field[:, :, :3], 'lat', [(i + 1, i) for i in range(count - 1)])  5.46 us
    sub x5, other arithmetic, ppm_sweep(): 7.0 / 12.0 * (piece(1, count + 4) + piece(2, count + 5))  4.44 us
  transfers between devices with their start and end apart: 5, of which 3 were waited for; matrix products, arithmetic and copies ran while one was open for 5% of the time, Pallas kernels for 0%

profile of v4, /device:TPU:7, one launch (start us, length us, event | category | flops | bytes accessed | tf_op | source)
XLA Modules:
  0.0 196.3 jit_solution(13910772669234554326)
XLA Ops:
  0.0 0.9 fusion.150
  0.9 1.3 concatenate.104
  5.8 3.7 %collective-permute-start = (f32[4,2,3,2880]{3,2,1,0:T(4,128)S(1)}, f32[4,2,3,2880]{3,2,1,0:T(4,128)S(1)}, u32[]{:S(2)}, u32[]{:S(2)}) collective-permute-start(f32[4,2,3,2880]{3,2,1,0:T(4,128)S(1)} %pad_maximum_fusion.3), channel_id=1, source_target_pairs={{0,32},{32,64},{64,96},{96,128},{128,160},{160,192},{192,224},{224... | collective-permute-start | bytes 829448 | tf_op jit(solution)/shard_map/ppermute | solution.py:107
  10.2 1.9 collective-permute-start.1
  12.2 0.8 broadcast_compare_fusion.2
  13.0 0.8 broadcast_multiply_fusion.3
  15.0 5.5 %collective-permute-done.1 = f32[3,2,3,2880]{3,2,1,0:T(4,128)S(1)} collective-permute-done((f32[3,2,3,2880]{3,2,1,0:T(4,128)}, f32[3,2,3,2880]{3,2,1,0:T(4,128)S(1)}, u32[]{:S(2)}, u32[]{:S(2)}) %collective-permute-start.1) | collective-permute-done | bytes 207392 | tf_op jit(solution)/shard_map/ppermute | solution.py:108
  24.1 1.0 concatenate.120
  25.1 1.7 fusion.100
  29.2 1.2 fusion.101
  30.4 1.9 collective-permute-start.2
  32.3 2.6 %collective-permute-start.3 = (f32[3,2,3,2880]{3,2,1,0:T(4,128)}, f32[3,2,3,2880]{3,2,1,0:T(4,128)S(1)}, u32[]{:S(2)}, u32[]{:S(2)}) collective-permute-start(f32[3,2,3,2880]{3,2,1,0:T(4,128)} %get-tuple-element.50), channel_id=1, source_target_pairs={{32,0},{64,32},{96,64},{128,96},{160,128},{192,160},{224,192},{256... | collective-permute-start | bytes 622088 | tf_op jit(solution)/shard_map/ppermute | solution.py:118
  34.9 1.1 concatenate.112
  36.0 1.3 fusion.37
  39.1 3.4 %collective-permute-done.3 = f32[3,2,3,2880]{3,2,1,0:T(4,128)S(1)} collective-permute-done((f32[3,2,3,2880]{3,2,1,0:T(4,128)}, f32[3,2,3,2880]{3,2,1,0:T(4,128)S(1)}, u32[]{:S(2)}, u32[]{:S(2)}) %collective-permute-start.3) | collective-permute-done | bytes 207392 | tf_op jit(solution)/shard_map/ppermute | solution.py:118
  44.4 1.4 reshape.203
  46.2 2.2 %all_to_all.16 = f32[32,1,4320]{2,1,0:T(1,128)} reshape(f32[32,3,2,8,90]{4,3,2,1,0:T(8,128)S(1)} %bitcast.26) | data formatting | bytes 1105920 | tf_op jit(solution)/shard_map/all_to_all | solution.py:124
  48.4 28.8 %all-to-all-start = ((f32[32,1,4320]{2,1,0:T(1,128)}), f32[32,1,4320]{2,1,0:T(1,128)S(1)}, u32[]{:S(2)}, u32[]{:S(2)}) async-start(f32[32,1,4320]{2,1,0:T(1,128)} %all_to_all.16), calls=%async_computation | async-start | bytes 1114112 | tf_op jit(solution)/shard_map/all_to_all | solution.py:124
  77.4 1.6 fusion.115
  80.0 62.3 %all-to-all-done = f32[32,1,4320]{2,1,0:T(1,128)S(1)} async-done(((f32[32,1,4320]{2,1,0:T(1,128)}), f32[32,1,4320]{2,1,0:T(1,128)S(1)}, u32[]{:S(2)}, u32[]{:S(2)}) %all-to-all-start) | async-done | bytes 552992 | tf_op jit(solution)/shard_map/all_to_all | solution.py:124
  142.3 1.3 reduce
  144.5 2.0 %fusion.56 = f32[32,3,8,90]{3,2,0,1:T(8,128)S(1)} fusion(f32[3,64,8,90]{3,2,1,0:T(8,128)S(1)} %broadcast_multiply_fusion, f32[32,8,90]{2,1,0:T(8,128)S(1)} %copy.154, pred[32,8,90]{2,1,0:T(8,128)(4,1)S(1)} %copy.153, pred[32,8,90]{2,1,0:T(8,128)(4,1)S(1)} %copy.152, pred[32,8,90]{2,1,0:T(8,128)(4,1)S(1)} %copy.151, pred[32,8,90]{2,1,0:T(8,128)(4,1)S(1)} %copy.150, ...), kind=kLoop, calls=%fused_computation.88 | loop fusion | flops 4561920 | bytes 10252800 | tf_op jit(solution)/shard_map/transpose | solution.py:87
  147.0 47.3 %all_to_all.20 = f32[32,1,2160]{2,1,0:T(1,128)S(1)} all-to-all(f32[32,1,2160]{2,1,0:T(1,128)S(1)} %all_to_all.17), channel_id=1, replica_groups=mesh['lat'=32,'lev'=32] {'lev'}, dimensions={0} | all-to-all | bytes 552960 | tf_op jit(solution)/shard_map/all_to_all | solution.py:129
  195.3 1.0 reshape.207
  (133 shorter events, 18.6 us)
Async XLA Ops:
  0.0 2.2 %copy-start.2 = (f32[3,2,8,2880]{3,2,1,0:T(8,128)S(1)}, f32[3,2,8,2880]{3,2,1,0:T(8,128)}, u32[]{:S(2)}) copy-start(f32[3,2,8,2880]{3,2,1,0:T(8,128)} %param.5) | copy-start | bytes 1658884
  2.8 0.9 copy-start.14
  5.8 8.8 %collective-permute-start = (f32[4,2,3,2880]{3,2,1,0:T(4,128)S(1)}, f32[4,2,3,2880]{3,2,1,0:T(4,128)S(1)}, u32[]{:S(2)}, u32[]{:S(2)}) collective-permute-start(f32[4,2,3,2880]{3,2,1,0:T(4,128)S(1)} %pad_maximum_fusion.3), channel_id=1, source_target_pairs={{0,32},{32,64},{64,96},{96,128},{128,160},{160,192},{192,224},{224... | collective-permute-start | bytes 829448 | tf_op jit(solution)/shard_map/ppermute | solution.py:107
  10.2 10.2 %collective-permute-start.1 = (f32[3,2,3,2880]{3,2,1,0:T(4,128)}, f32[3,2,3,2880]{3,2,1,0:T(4,128)S(1)}, u32[]{:S(2)}, u32[]{:S(2)}) collective-permute-start(f32[3,2,3,2880]{3,2,1,0:T(4,128)} %slice.828), channel_id=1, source_target_pairs={{32,0},{64,32},{96,64},{128,96},{160,128},{192,160},{224,192},{256... | collective-permute-start | bytes 622088 | tf_op jit(solution)/shard_map/ppermute | solution.py:108
  13.0 1.5 copy-start.12
  13.0 1.7 copy-start.10
  23.0 1.0 copy-start.21
  26.8 0.9 copy-start.18
  26.8 1.0 copy-start.19
  26.8 1.0 copy-start.20
  26.9 1.0 copy-start.23
  27.6 0.9 copy-start.11
  27.6 1.0 copy-start.15
  27.6 1.0 copy-start.16
  27.6 1.0 copy-start.17
  27.7 1.0 copy-start.22
  30.4 8.7 %collective-permute-start.2 = (f32[3,2,3,2880]{3,2,1,0:T(4,128)}, f32[3,2,3,2880]{3,2,1,0:T(4,128)S(1)}, u32[]{:S(2)}, u32[]{:S(2)}) collective-permute-start(f32[3,2,3,2880]{3,2,1,0:T(4,128)} %get-tuple-element.49), channel_id=1, source_target_pairs={{0,32},{32,64},{64,96},{96,128},{128,160},{160,192},{192,224},{224... | collective-permute-start | bytes 622088 | tf_op jit(solution)/shard_map/ppermute | solution.py:113
  32.3 10.2 %collective-permute-start.3 = (f32[3,2,3,2880]{3,2,1,0:T(4,128)}, f32[3,2,3,2880]{3,2,1,0:T(4,128)S(1)}, u32[]{:S(2)}, u32[]{:S(2)}) collective-permute-start(f32[3,2,3,2880]{3,2,1,0:T(4,128)} %get-tuple-element.50), channel_id=1, source_target_pairs={{32,0},{64,32},{96,64},{128,96},{160,128},{192,160},{224,192},{256... | collective-permute-start | bytes 622088 | tf_op jit(solution)/shard_map/ppermute | solution.py:118
  37.2 0.9 copy-start.4
  37.2 1.0 copy-start.6
  37.2 1.1 copy-start.8
  46.2 31.0 %copy-start = (f32[8,90,64]{1,2,0:T(8,128)S(1)}, f32[8,90,64]{1,2,0:T(8,128)}, u32[]{:S(2)}) copy-start(f32[8,90,64]{1,2,0:T(8,128)} %param.8) | copy-start | bytes 552964
  48.4 29.0 %copy-start.1 = (s32[8,90,64]{1,2,0:T(8,128)S(1)}, s32[8,90,64]{1,2,0:T(8,128)}, u32[]{:S(2)}) copy-start(s32[8,90,64]{1,2,0:T(8,128)} %param.9) | copy-start | bytes 552964
  48.4 94.0 %all-to-all-start = ((f32[32,1,4320]{2,1,0:T(1,128)}), f32[32,1,4320]{2,1,0:T(1,128)S(1)}, u32[]{:S(2)}, u32[]{:S(2)}) async-start(f32[32,1,4320]{2,1,0:T(1,128)} %all_to_all.16), calls=%async_computation | async-start | bytes 1114112 | tf_op jit(solution)/shard_map/all_to_all | solution.py:124
  (5 other events, 4.0 us)

commit v5 on v3

--- a/solution.py
+++ b/solution.py
@@ -61,6 +61,7 @@
     count = field.shape[-1]
     padded = jnp.concatenate([field[..., -3:], field, field[..., :3]], axis=-1)
     faces = jnp.concatenate([courant_x[..., -1:], courant_x], axis=-1)
+    faces = lax.optimization_barrier(faces)
     return ppm_sweep(padded, faces, 3, count)
 
 

time: 192 us -> 191 us (level)
  no operation moved by 1% of the time
where the time goes in v5:
time: 191 us
  waiting for transfers between devices  76.2 us (40%)
  blocking collectives  47.1 us (25%)
  starting transfers between devices  38.7 us (20%)
  other arithmetic  14.7 us (8%)
  local copies, waits for them, and re-layouts  13.5 us (7%)
    all_to_all x1, waiting for transfers between devices, local(): lax.all_to_all(blocks.reshape(parts, -1), 'lev', split_axis=0, concat_axi...  62.2 us
    all_to_all x1, blocking collectives, local(): lax.all_to_all(out.reshape(parts, -1), 'lev', split_axis=0, concat_axis=0...  47.1 us
    all_to_all x1, starting transfers between devices, local(): lax.all_to_all(blocks.reshape(parts, -1), 'lev', split_axis=0, concat_axi...  28.8 us
    ppermute x1, waiting for transfers between devices, padded_2(): lax.ppermute(head, axis, [((i + 1) % count, i) for i in range(ends)])  6.51 us
    ppermute x1, waiting for transfers between devices, local(): lax.ppermute(field[:, :, :3], 'lat', [(i + 1, i) for i in range(count - 1)])  4.61 us
  transfers between devices with their start and end apart: 5, of which 5 were waited for; matrix products, arithmetic and copies ran while one was open for 2% of the time, Pallas kernels for 0%

profile of v5, /device:TPU:7, one launch (start us, length us, event | category | flops | bytes accessed | tf_op | source)
XLA Modules:
  0.0 190.9 jit_solution(7428445506076322583)
XLA Ops:
  0.0 0.8 slice.507
  0.8 1.0 pad_maximum_fusion.4
  4.8 3.7 %collective-permute-start = (f32[4,2,3,2880]{3,2,1,0:T(4,128)S(1)}, f32[4,2,3,2880]{3,2,1,0:T(4,128)S(1)}, u32[]{:S(2)}, u32[]{:S(2)}) collective-permute-start(f32[4,2,3,2880]{3,2,1,0:T(4,128)S(1)} %pad_maximum_fusion.3), channel_id=1, source_target_pairs={{0,32},{32,64},{64,96},{96,128},{128,160},{160,192},{192,224},{224... | collective-permute-start | bytes 829448 | tf_op jit(solution)/shard_map/ppermute | solution.py:107
  8.5 0.7 slice.680
  9.2 1.9 collective-permute-start.1
  11.2 1.8 collective-permute-done
  13.0 0.8 copy-done.5
  14.8 4.6 %collective-permute-done.1 = f32[3,2,3,2880]{3,2,1,0:T(4,128)S(1)} collective-permute-done((f32[3,2,3,2880]{3,2,1,0:T(4,128)}, f32[3,2,3,2880]{3,2,1,0:T(4,128)S(1)}, u32[]{:S(2)}, u32[]{:S(2)}) %collective-permute-start.1) | collective-permute-done | bytes 207392 | tf_op jit(solution)/shard_map/ppermute | solution.py:108
  22.0 1.1 concatenate.55
  23.0 1.3 fusion.37
  25.5 1.9 %collective-permute-start.2 = (f32[3,2,3,2880]{3,2,1,0:T(4,128)S(1)}, f32[3,2,3,2880]{3,2,1,0:T(4,128)S(1)}, u32[]{:S(2)}, u32[]{:S(2)}) collective-permute-start(f32[3,2,3,2880]{3,2,1,0:T(4,128)S(1)} %get-tuple-element.43), channel_id=1, source_target_pairs={{0,32},{32,64},{64,96},{96,128},{128,160},{160,192},{192,224},{224... | collective-permute-start | bytes 622088 | tf_op jit(solution)/shard_map/ppermute | solution.py:17
  27.5 2.4 %collective-permute-start.3 = (f32[3,2,3,2880]{3,2,1,0:T(4,128)S(1)}, f32[3,2,3,2880]{3,2,1,0:T(4,128)S(1)}, u32[]{:S(2)}, u32[]{:S(2)}) collective-permute-start(f32[3,2,3,2880]{3,2,1,0:T(4,128)S(1)} %get-tuple-element.44), channel_id=1, source_target_pairs={{32,0},{64,32},{96,64},{128,96},{160,128},{192,160},{224,192},{256... | collective-permute-start | bytes 622088 | tf_op jit(solution)/shard_map/ppermute | solution.py:19
  29.9 1.1 collective-permute-done.2
  31.0 6.5 %collective-permute-done.3 = f32[3,2,3,2880]{3,2,1,0:T(4,128)S(1)} collective-permute-done((f32[3,2,3,2880]{3,2,1,0:T(4,128)S(1)}, f32[3,2,3,2880]{3,2,1,0:T(4,128)S(1)}, u32[]{:S(2)}, u32[]{:S(2)}) %collective-permute-start.3) | collective-permute-done | bytes 207392 | tf_op jit(solution)/shard_map/ppermute | solution.py:19
  39.3 1.4 reshape.84
  41.2 2.2 %all_to_all.16 = f32[32,1,4320]{2,1,0:T(1,128)} reshape(f32[32,3,2,8,90]{4,3,2,1,0:T(8,128)S(1)} %bitcast.26) | data formatting | bytes 1105920 | tf_op jit(solution)/shard_map/all_to_all | solution.py:115
  43.3 28.8 %all-to-all-start = ((f32[32,1,4320]{2,1,0:T(1,128)}), f32[32,1,4320]{2,1,0:T(1,128)S(1)}, u32[]{:S(2)}, u32[]{:S(2)}) async-start(f32[32,1,4320]{2,1,0:T(1,128)} %all_to_all.16), calls=%async_computation | async-start | bytes 1114112 | tf_op jit(solution)/shard_map/all_to_all | solution.py:115
  72.3 1.6 fusion.89
  74.9 62.2 %all-to-all-done = f32[32,1,4320]{2,1,0:T(1,128)S(1)} async-done(((f32[32,1,4320]{2,1,0:T(1,128)}), f32[32,1,4320]{2,1,0:T(1,128)S(1)}, u32[]{:S(2)}, u32[]{:S(2)}) %all-to-all-start) | async-done | bytes 552992 | tf_op jit(solution)/shard_map/all_to_all | solution.py:115
  137.1 1.3 reduce
  138.4 0.7 reshape.85
  139.3 2.0 %fusion.56 = f32[32,3,8,90]{3,2,0,1:T(8,128)S(1)} fusion(f32[3,64,8,90]{3,2,1,0:T(8,128)S(1)} %broadcast_multiply_fusion, f32[32,8,90]{2,1,0:T(8,128)S(1)} %copy.154, pred[32,8,90]{2,1,0:T(8,128)(4,1)S(1)} %copy.153, pred[32,8,90]{2,1,0:T(8,128)(4,1)S(1)} %copy.152, pred[32,8,90]{2,1,0:T(8,128)(4,1)S(1)} %copy.151, pred[32,8,90]{2,1,0:T(8,128)(4,1)S(1)} %copy.150, ...), kind=kLoop, calls=%fused_computation.88 | loop fusion | flops 4561920 | bytes 10252800 | tf_op jit(solution)/shard_map/transpose | solution.py:88
  141.8 47.1 %all_to_all.20 = f32[32,1,2160]{2,1,0:T(1,128)S(1)} all-to-all(f32[32,1,2160]{2,1,0:T(1,128)S(1)} %all_to_all.17), channel_id=1, replica_groups=mesh['lat'=32,'lev'=32] {'lev'}, dimensions={0} | all-to-all | bytes 552960 | tf_op jit(solution)/shard_map/all_to_all | solution.py:120
  190.0 1.0 reshape.88
  (86 shorter events, 12.4 us)
Async XLA Ops:
  0.0 2.0 %copy-start.2 = (f32[3,2,8,2880]{3,2,1,0:T(8,128)S(1)}, f32[3,2,8,2880]{3,2,1,0:T(8,128)}, u32[]{:S(2)}) copy-start(f32[3,2,8,2880]{3,2,1,0:T(8,128)} %param.5) | copy-start | bytes 1658884
  3.8 0.9 copy-start.3
  4.0 9.8 %copy-start.4 = (f32[2,8,2880]{2,1,0:T(8,128)S(1)}, f32[2,8,2880]{2,1,0:T(8,128)}, u32[]{:S(2)}) copy-start(f32[2,8,2880]{2,1,0:T(8,128)} %param.7) | copy-start | bytes 552964
  4.8 8.2 %collective-permute-start = (f32[4,2,3,2880]{3,2,1,0:T(4,128)S(1)}, f32[4,2,3,2880]{3,2,1,0:T(4,128)S(1)}, u32[]{:S(2)}, u32[]{:S(2)}) collective-permute-start(f32[4,2,3,2880]{3,2,1,0:T(4,128)S(1)} %pad_maximum_fusion.3), channel_id=1, source_target_pairs={{0,32},{32,64},{64,96},{96,128},{128,160},{160,192},{192,224},{224... | collective-permute-start | bytes 829448 | tf_op jit(solution)/shard_map/ppermute | solution.py:107
  9.2 10.2 %collective-permute-start.1 = (f32[3,2,3,2880]{3,2,1,0:T(4,128)}, f32[3,2,3,2880]{3,2,1,0:T(4,128)S(1)}, u32[]{:S(2)}, u32[]{:S(2)}) collective-permute-start(f32[3,2,3,2880]{3,2,1,0:T(4,128)} %slice.680), channel_id=1, source_target_pairs={{32,0},{64,32},{96,64},{128,96},{160,128},{192,160},{224,192},{256... | collective-permute-start | bytes 622088 | tf_op jit(solution)/shard_map/ppermute | solution.py:108
  13.0 0.8 copy-start.5
  13.8 1.0 copy-start.6
  25.5 5.4 %collective-permute-start.2 = (f32[3,2,3,2880]{3,2,1,0:T(4,128)S(1)}, f32[3,2,3,2880]{3,2,1,0:T(4,128)S(1)}, u32[]{:S(2)}, u32[]{:S(2)}) collective-permute-start(f32[3,2,3,2880]{3,2,1,0:T(4,128)S(1)} %get-tuple-element.43), channel_id=1, source_target_pairs={{0,32},{32,64},{64,96},{96,128},{128,160},{160,192},{192,224},{224... | collective-permute-start | bytes 622088 | tf_op jit(solution)/shard_map/ppermute | solution.py:17
  27.5 10.0 %collective-permute-start.3 = (f32[3,2,3,2880]{3,2,1,0:T(4,128)S(1)}, f32[3,2,3,2880]{3,2,1,0:T(4,128)S(1)}, u32[]{:S(2)}, u32[]{:S(2)}) collective-permute-start(f32[3,2,3,2880]{3,2,1,0:T(4,128)S(1)} %get-tuple-element.44), channel_id=1, source_target_pairs={{32,0},{64,32},{96,64},{128,96},{160,128},{192,160},{224,192},{256... | collective-permute-start | bytes 622088 | tf_op jit(solution)/shard_map/ppermute | solution.py:19
  41.2 30.9 %copy-start = (f32[8,90,64]{1,2,0:T(8,128)S(1)}, f32[8,90,64]{1,2,0:T(8,128)}, u32[]{:S(2)}) copy-start(f32[8,90,64]{1,2,0:T(8,128)} %param.8) | copy-start | bytes 552964
  43.3 28.9 %copy-start.1 = (s32[8,90,64]{1,2,0:T(8,128)S(1)}, s32[8,90,64]{1,2,0:T(8,128)}, u32[]{:S(2)}) copy-start(s32[8,90,64]{1,2,0:T(8,128)} %param.9) | copy-start | bytes 552964
  43.3 93.8 %all-to-all-start = ((f32[32,1,4320]{2,1,0:T(1,128)}), f32[32,1,4320]{2,1,0:T(1,128)S(1)}, u32[]{:S(2)}, u32[]{:S(2)}) async-start(f32[32,1,4320]{2,1,0:T(1,128)} %all_to_all.16), calls=%async_computation | async-start | bytes 1114112 | tf_op jit(solution)/shard_map/all_to_all | solution.py:115
